TPU v7x, 128 devices: a whole 4x4x4 slice. The times are simulated.
128 devices in a mesh: ctx: 16 (over z, y), head: 8 (over x, core).
Axes of the slice: x: 4, y: 4, z: 4, core: 2. Of those that a mesh axis runs over, the one named last changes fastest.
Arguments:
- queries: bfloat16 [16384, 8192], P(('ctx', 'head')), may hold values from -200 to 200
- keys: bfloat16 [16384, 1024], P(('ctx', 'head')), may hold values from -6 to 6
- values: bfloat16 [16384, 1024], P(('ctx', 'head')), may hold values from -6 to 6
- doc_lengths: int32 [8], replicated, may hold values from 1 to 3073, 16384 in all
Outputs:
- attended: bfloat16 [16384, 8192], P(('ctx', 'head'))
All inputs are finite; a program needn't handle non-finite values.
Results may differ from a plain program's by a relative error of at most 0.0024.
Values may be sent and summed in bfloat16 or wider, within the bound.
No kernel may reach another device: no remote copies, remote signals or barrier semaphores. Data moves between devices by JAX's collectives and lax.ppermute only.
A program may use at most 256 MiB of HBM per device.

v0:
```python
import functools
import math

import jax
import jax.numpy as jnp
from jax import lax
from jax.experimental import pallas as pl
from jax.experimental.pallas import tpu as pltpu
from jax.sharding import PartitionSpec as P

HD = 128
REACH = 3
Q_BLOCK = 256
K_BLOCK = 2048

MASK_FILL = -1e30


def shifted(block, axis, distance):
    devices = range(lax.axis_size(axis))
    route = [(i - distance, i) for i in devices if i - distance in devices]
    return lax.ppermute(block, axis, route)


def doc_first(positions, doc_starts):
    return jnp.max(
        jnp.where(positions[:, None] >= doc_starts[None, :], doc_starts[None, :], 0), axis=1
    )


def attention_kernel(
    table_ref, q_ref, k_ref, v_ref, low_ref, o_ref, top_sc, sum_sc, acc_sc, *, groups
):
    i = pl.program_id(0)
    j = pl.program_id(1)
    tq = q_ref.shape[0]
    tk = k_ref.shape[0]
    q_base = table_ref[0]
    k_base = table_ref[1]
    need_lo = table_ref[2 + 4 * i]
    need_hi = table_ref[3 + 4 * i]
    full_lo = table_ref[4 + 4 * i]
    full_hi = table_ref[5 + 4 * i]

    @pl.when(j == 0)
    def _():
        top_sc[...] = jnp.full(top_sc.shape, MASK_FILL, jnp.float32)
        sum_sc[...] = jnp.zeros(sum_sc.shape, jnp.float32)
        acc_sc[...] = jnp.zeros(acc_sc.shape, jnp.float32)

    needed = (j >= need_lo) & (j <= need_hi)
    full = (j >= full_lo) & (j <= full_hi)

    def step(masked):
        k = k_ref[...]
        v = v_ref[...]
        if masked:
            q_pos = q_base + i * tq + lax.broadcasted_iota(jnp.int32, (tq, tk), 0)
            k_pos = k_base + j * tk + lax.broadcasted_iota(jnp.int32, (tq, tk), 1)
            allowed = (k_pos <= q_pos) & (k_pos >= low_ref[...])
        for h in range(groups):
            q = q_ref[:, h * HD : (h + 1) * HD]
            scores = lax.dot_general(
                q, k, (((1,), (1,)), ((), ())), preferred_element_type=jnp.float32
            ) * HD ** (-0.5)
            if masked:
                scores = jnp.where(allowed, scores, MASK_FILL)
            top_old = top_sc[h]
            top_new = jnp.maximum(top_old, jnp.max(scores, axis=1, keepdims=True))
            weights = jnp.exp(scores - top_new)
            if masked:
                weights = jnp.where(allowed, weights, 0.0)
            rescale = jnp.exp(top_old - top_new)
            sum_sc[h] = sum_sc[h] * rescale + jnp.sum(weights, axis=1, keepdims=True)
            update = lax.dot_general(
                weights.astype(jnp.bfloat16),
                v,
                (((1,), (0,)), ((), ())),
                preferred_element_type=jnp.float32,
            )
            acc_sc[h] = acc_sc[h] * rescale + update
            top_sc[h] = top_new

    @pl.when(needed & full)
    def _():
        step(False)

    @pl.when(needed & jnp.logical_not(full))
    def _():
        step(True)

    @pl.when(j == pl.num_programs(1) - 1)
    def _():
        for h in range(groups):
            o_ref[:, h * HD : (h + 1) * HD] = (acc_sc[h] / sum_sc[h]).astype(o_ref.dtype)


def attend(q_loc, kv_all, row_low, q_base, k_base):
    tokens, q_width = q_loc.shape
    span = kv_all.shape[0]
    groups = q_width // HD
    tq = min(Q_BLOCK, tokens)
    tk = min(K_BLOCK, span)
    nq = tokens // tq
    nk = span // tk
    firsts = q_base + jnp.arange(nq, dtype=jnp.int32) * tq
    lasts = firsts + tq - 1
    low_min = row_low[::tq]
    low_max = row_low[tq - 1 :: tq]
    need_lo = jnp.maximum((low_min - k_base) // tk, 0)
    need_hi = jnp.minimum((lasts - k_base) // tk, nk - 1)
    full_lo = -((k_base - low_max) // tk)
    full_hi = (firsts + 1 - k_base) // tk - 1
    per_block = jnp.stack([need_lo, need_hi, full_lo, full_hi], axis=1).reshape(-1)
    table = jnp.concatenate(
        [jnp.stack([q_base, k_base]).astype(jnp.int32), per_block.astype(jnp.int32)]
    )

    def kv_index(col):
        def index(i, j, table_ref):
            lo = table_ref[2 + 4 * i]
            hi = table_ref[3 + 4 * i]
            return (jnp.minimum(jnp.maximum(j, lo), hi), col)

        return index

    grid_spec = pltpu.PrefetchScalarGridSpec(
        num_scalar_prefetch=1,
        grid=(nq, nk),
        in_specs=[
            pl.BlockSpec((tq, q_width), lambda i, j, t: (i, 0)),
            pl.BlockSpec((tk, HD), kv_index(0)),
            pl.BlockSpec((tk, HD), kv_index(1)),
            pl.BlockSpec((tq, 1), lambda i, j, t: (i, 0)),
        ],
        out_specs=pl.BlockSpec((tq, q_width), lambda i, j, t: (i, 0)),
        scratch_shapes=[
            pltpu.VMEM((groups, tq, 1), jnp.float32),
            pltpu.VMEM((groups, tq, 1), jnp.float32),
            pltpu.VMEM((groups, tq, HD), jnp.float32),
        ],
    )
    return pl.pallas_call(
        functools.partial(attention_kernel, groups=groups),
        grid_spec=grid_spec,
        out_shape=jax.ShapeDtypeStruct((tokens, q_width), jnp.bfloat16),
        compiler_params=pltpu.CompilerParams(
            dimension_semantics=("arbitrary", "arbitrary")
        ),
    )(table, q_loc, kv_all, kv_all, row_low.reshape(tokens, 1))


def shards(queries, keys, values, doc_lengths):
    rows = keys.shape[0]
    heads = keys.shape[1] // HD
    kv_pairs = jnp.concatenate(
        [keys.reshape(rows, heads, HD), values.reshape(rows, heads, HD)], axis=2
    )
    kv_loc = lax.all_to_all(kv_pairs, "head", split_axis=1, concat_axis=0, tiled=True)
    kv_loc = kv_loc.reshape(kv_loc.shape[0], 2 * HD)
    q_loc = lax.all_to_all(
        queries.reshape(rows, heads, -1), "head", split_axis=1, concat_axis=0, tiled=True
    )
    q_loc = q_loc.reshape(q_loc.shape[0], -1)
    my_index = lax.axis_index("ctx")
    tokens = q_loc.shape[0]
    doc_ends = jnp.cumsum(doc_lengths)
    doc_starts = doc_ends - doc_lengths
    row_pos = my_index * tokens + jnp.arange(tokens, dtype=jnp.int32)
    row_low = doc_first(row_pos, doc_starts).astype(jnp.int32)
    pieces = [kv_loc]
    for distance in range(1, REACH + 1):
        pieces.append(shifted(kv_loc, "ctx", distance))
    kv_all = jnp.concatenate(pieces[::-1], axis=0)
    q_base = (my_index * tokens).astype(jnp.int32)
    k_base = ((my_index - REACH) * tokens).astype(jnp.int32)
    owned = attend(q_loc, kv_all, row_low, q_base, k_base)
    back = lax.all_to_all(
        owned.reshape(heads, rows, -1), "head", split_axis=0, concat_axis=0, tiled=True
    )
    return jnp.transpose(back, (1, 0, 2)).reshape(rows, -1)


def solution(mesh):
    return jax.shard_map(
        shards,
        mesh=mesh,
        in_specs=(
            P(("ctx", "head"), None),
            P(("ctx", "head"), None),
            P(("ctx", "head"), None),
            P(),
        ),
        out_specs=P(("ctx", "head"), None),
        check_vma=False,
    )
```

profile of v0, /device:TPU:32, one launch (start us, length us, event | category | flops | bytes accessed | tf_op | source)
XLA Modules:
  0.0 181.7 jit_solution(840553566443817468)
XLA Ops:
  0.0 0.0 copy-start
  0.0 0.0 copy-start.2
  0.0 0.9 copy-done
  1.0 1.1 copy_bitcast_fusion.1
  2.0 0.9 pad_maximum_fusion.1
  2.9 4.3 %all-to-all-start.1 = ((bf16[128,8,256]{2,0,1:T(8,128)(2,1)}), bf16[128,8,256]{2,0,1:T(8,128)(2,1)S(1)}, u32[]{:S(2)}, u32[]{:S(2)}) async-start(bf16[128,8,256]{2,0,1:T(8,128)(2,1)} %pad_maximum_fusion.1), calls=%async_computation.1 | async-start | bytes 1048576 | tf_op jit(solution)/shard_map/all_to_all | solution.py:159
  7.2 0.0 copy-done.2
  7.2 1.6 copy.29
  8.8 8.8 %all-to-all-done.1 = bf16[128,8,256]{2,0,1:T(8,128)(2,1)S(1)} async-done(((bf16[128,8,256]{2,0,1:T(8,128)(2,1)}), bf16[128,8,256]{2,0,1:T(8,128)(2,1)S(1)}, u32[]{:S(2)}, u32[]{:S(2)}) %all-to-all-start.1) | async-done | bytes 524320 | tf_op jit(solution)/shard_map/all_to_all | solution.py:159
  17.5 0.0 copy-start.3
  17.5 3.7 %all-to-all-start = ((bf16[128,8,1024]{2,0,1:T(8,128)(2,1)}), bf16[128,8,1024]{2,0,1:T(8,128)(2,1)S(1)}, u32[]{:S(2)}, u32[]{:S(2)}) async-start(bf16[128,8,1024]{2,0,1:T(8,128)(2,1)} %bitcast.40), calls=%async_computation | async-start | bytes 4194304 | tf_op jit(solution)/shard_map/all_to_all | solution.py:161
  21.3 0.0 copy-done.3
  21.3 0.2 reduce-window.9
  21.5 0.1 select_reduce_fusion
  21.6 0.1 slice.7
  21.7 0.1 slice.6
  21.8 3.5 %collective-permute-start.2 = (bf16[1024,256]{1,0:T(8,128)(2,1)S(1)}, bf16[1024,256]{1,0:T(8,128)(2,1)S(1)}, u32[]{:S(2)}, u32[]{:S(2)}) collective-permute-start(bf16[1024,256]{1,0:T(8,128)(2,1)S(1)} %bitcast.43), channel_id=1, source_target_pairs={{0,8},{8,16},{16,24},{24,32},{32,40},{40,48},{48,56},{56,64},{64,7... | collective-permute-start | bytes 1572872 | tf_op jit(solution)/shard_map/ppermute | solution.py:22
  25.3 4.8 %collective-permute-start.1 = (bf16[1024,256]{1,0:T(8,128)(2,1)S(1)}, bf16[1024,256]{1,0:T(8,128)(2,1)}, u32[]{:S(2)}, u32[]{:S(2)}) collective-permute-start(bf16[1024,256]{1,0:T(8,128)(2,1)S(1)} %bitcast.44), channel_id=1, source_target_pairs={{0,16},{8,24},{16,32},{24,40},{32,48},{40,56},{48,64},{56,72},{64,... | collective-permute-start | bytes 1572872 | tf_op jit(solution)/shard_map/ppermute | solution.py:22
  30.1 4.6 %collective-permute-start = (bf16[1024,256]{1,0:T(8,128)(2,1)S(1)}, bf16[1024,256]{1,0:T(8,128)(2,1)}, u32[]{:S(2)}, u32[]{:S(2)}) collective-permute-start(bf16[1024,256]{1,0:T(8,128)(2,1)S(1)} %bitcast.45), channel_id=1, source_target_pairs={{0,24},{8,32},{16,40},{24,48},{32,56},{40,64},{48,72},{56,80},{64,... | collective-permute-start | bytes 1572872 | tf_op jit(solution)/shard_map/ppermute | solution.py:22
  34.8 0.1 copy.16
  34.9 0.1 reshape.181
  35.0 1.0 copy.20.low_ref
  36.0 0.7 pad_add_fusion.1.table_ref
  36.7 20.3 %collective-permute-done.2 = bf16[1024,256]{1,0:T(8,128)(2,1)S(1)} collective-permute-done((bf16[1024,256]{1,0:T(8,128)(2,1)S(1)}, bf16[1024,256]{1,0:T(8,128)(2,1)S(1)}, u32[]{:S(2)}, u32[]{:S(2)}) %collective-permute-start.2) | collective-permute-done | bytes 524320 | tf_op jit(solution)/shard_map/ppermute | solution.py:22
  56.9 0.0 collective-permute-done.1
  56.9 5.6 %collective-permute-done = bf16[1024,256]{1,0:T(8,128)(2,1)} collective-permute-done((bf16[1024,256]{1,0:T(8,128)(2,1)S(1)}, bf16[1024,256]{1,0:T(8,128)(2,1)}, u32[]{:S(2)}, u32[]{:S(2)}) %collective-permute-start) | collective-permute-done | bytes 524320 | tf_op jit(solution)/shard_map/ppermute | solution.py:22
  62.6 2.7 %pad_maximum_fusion.k_ref.v_ref = bf16[4096,256]{1,0:T(8,128)(2,1)} fusion(bf16[1024,256]{1,0:T(8,128)(2,1)S(1)} %bitcast.46, bf16[1024,256]{1,0:T(8,128)(2,1)S(1)} %collective-permute-done.2, bf16[1024,256]{1,0:T(8,128)(2,1)} %collective-permute-done.1, bf16[1024,256]{1,0:T(8,128)(2,1)} %collective-permute-done), kind=kLoop, calls=%fused_computation.1 | loop fusion | flops 8388608 | bytes 4194304 | tf_op jit(solution)/shard_map/concatenate | solution.py:174
  65.2 0.0 all-to-all-done
  65.2 0.0 copy-start.1
  65.2 1.3 copy-done.1
  66.6 81.6 %shard_map.46 = bf16[1024,1024]{1,0:T(8,128)(2,1)} custom-call(s32[18]{0:T(128)} %pad_add_fusion.1.table_ref, bf16[1024,1024]{1,0:T(8,128)(2,1)} %bitcast.38, bf16[4096,256]{1,0:T(8,128)(2,1)} %pad_maximum_fusion.k_ref.v_ref, bf16[4096,256]{1,0:T(8,128)(2,1)} %pad_maximum_fusion.k_ref.v_ref, s32[1024,1]{1,0:T(8,128)} %copy.20.low_ref), custom_call_target="tpu_custom_call" | custom-call | tf_op jit(solution)/shard_map/pallas_call | solution.py:143
  148.2 32.0 %all_to_all.35 = bf16[8,128,1024]{2,1,0:T(8,128)(2,1)S(1)} all-to-all(bf16[8,128,1024]{2,1,0:T(8,128)(2,1)} %bitcast.39), channel_id=1, replica_groups=mesh['ctx'=16,'head'=8] {'head'}, dimensions={0} | all-to-all | bytes 4194304 | tf_op jit(solution)/shard_map/all_to_all | solution.py:178
  180.1 1.6 copy.25
  (5 shorter events, 0.0 us)
Async XLA Ops:
  0.0 1.0 copy-start
  0.0 7.2 %copy-start.2 = (bf16[128,8192]{1,0:T(8,128)(2,1)S(1)}, bf16[128,8192]{1,0:T(8,128)(2,1)}, u32[]{:S(2)}) copy-start(bf16[128,8192]{1,0:T(8,128)(2,1)} %param.4) | copy-start | bytes 6291460
  2.9 14.6 %all-to-all-start.1 = ((bf16[128,8,256]{2,0,1:T(8,128)(2,1)}), bf16[128,8,256]{2,0,1:T(8,128)(2,1)S(1)}, u32[]{:S(2)}, u32[]{:S(2)}) async-start(bf16[128,8,256]{2,0,1:T(8,128)(2,1)} %pad_maximum_fusion.1), calls=%async_computation.1 | async-start | bytes 1048576 | tf_op jit(solution)/shard_map/all_to_all | solution.py:159
  17.5 3.8 %copy-start.3 = (s32[8]{0:T(128)S(1)}, s32[8]{0:T(128)}, u32[]{:S(2)}) copy-start(s32[8]{0:T(128)} %param.7) | copy-start | bytes 100
  17.5 47.7 %all-to-all-start = ((bf16[128,8,1024]{2,0,1:T(8,128)(2,1)}), bf16[128,8,1024]{2,0,1:T(8,128)(2,1)S(1)}, u32[]{:S(2)}, u32[]{:S(2)}) async-start(bf16[128,8,1024]{2,0,1:T(8,128)(2,1)} %bitcast.40), calls=%async_computation | async-start | bytes 4194304 | tf_op jit(solution)/shard_map/all_to_all | solution.py:161
  21.8 35.2 %collective-permute-start.2 = (bf16[1024,256]{1,0:T(8,128)(2,1)S(1)}, bf16[1024,256]{1,0:T(8,128)(2,1)S(1)}, u32[]{:S(2)}, u32[]{:S(2)}) collective-permute-start(bf16[1024,256]{1,0:T(8,128)(2,1)S(1)} %bitcast.43), channel_id=1, source_target_pairs={{0,8},{8,16},{16,24},{24,32},{32,40},{40,48},{48,56},{56,64},{64,7... | collective-permute-start | bytes 1572872 | tf_op jit(solution)/shard_map/ppermute | solution.py:22
  25.3 31.7 %collective-permute-start.1 = (bf16[1024,256]{1,0:T(8,128)(2,1)S(1)}, bf16[1024,256]{1,0:T(8,128)(2,1)}, u32[]{:S(2)}, u32[]{:S(2)}) collective-permute-start(bf16[1024,256]{1,0:T(8,128)(2,1)S(1)} %bitcast.44), channel_id=1, source_target_pairs={{0,16},{8,24},{16,32},{24,40},{32,48},{40,56},{48,64},{56,72},{64,... | collective-permute-start | bytes 1572872 | tf_op jit(solution)/shard_map/ppermute | solution.py:22
  30.1 32.5 %collective-permute-start = (bf16[1024,256]{1,0:T(8,128)(2,1)S(1)}, bf16[1024,256]{1,0:T(8,128)(2,1)}, u32[]{:S(2)}, u32[]{:S(2)}) collective-permute-start(bf16[1024,256]{1,0:T(8,128)(2,1)S(1)} %bitcast.45), channel_id=1, source_target_pairs={{0,24},{8,32},{16,40},{24,48},{32,56},{40,64},{48,72},{56,80},{64,... | collective-permute-start | bytes 1572872 | tf_op jit(solution)/shard_map/ppermute | solution.py:22
  65.2 1.3 copy-start.1
where the time goes:
time: 182 us
  Pallas kernels  81.6 us (45%)
  waiting for transfers between devices  34.7 us (19%)
  blocking collectives  32 us (18%)
  starting transfers between devices  21 us (12%)
  local copies, waits for them, and re-layouts  7.87 us (4%)
  other arithmetic  4.53 us (2%)
    pallas_call x1, Pallas kernels, attend(): pl.pallas_call(functools.partial(attention_kernel, groups=groups), grid_s...  81.6 us
    all_to_all x1, blocking collectives, shards(): lax.all_to_all(owned.reshape(heads, rows, -1), 'head', split_axis=0, conc...  32 us
    ppermute x3, waiting for transfers between devices, shifted(): return lax.ppermute(block, axis, route)  25.9 us
    ppermute x3, starting transfers between devices, shifted(): return lax.ppermute(block, axis, route)  12.9 us
    all_to_all x1, waiting for transfers between devices, shards(): lax.all_to_all(kv_pairs, 'head', split_axis=1, concat_axis=0, tiled=True)  8.78 us
    all_to_all x1, starting transfers between devices, shards(): lax.all_to_all(kv_pairs, 'head', split_axis=1, concat_axis=0, tiled=True)  4.3 us
    all_to_all x1, starting transfers between devices, shards(): lax.all_to_all(queries.reshape(rows, heads, -1), 'head', split_axis=1, co...  3.74 us
  transfers between devices with their start and end apart: 5, of which 3 were waited for; matrix products, arithmetic and copies ran while one was open for 4% of the time, Pallas kernels for 0%

commit v1 on v0

--- a/solution.py
+++ b/solution.py
@@ -10,10 +10,11 @@
 
 HD = 128
 REACH = 3
-Q_BLOCK = 256
+Q_BLOCK = 512
 K_BLOCK = 2048
 
 MASK_FILL = -1e30
+EXP2_SCALE = HD ** (-0.5) * math.log2(math.e)
 
 
 def shifted(block, axis, distance):
@@ -58,19 +59,17 @@
             q_pos = q_base + i * tq + lax.broadcasted_iota(jnp.int32, (tq, tk), 0)
             k_pos = k_base + j * tk + lax.broadcasted_iota(jnp.int32, (tq, tk), 1)
             allowed = (k_pos <= q_pos) & (k_pos >= low_ref[...])
-        for h in range(groups):
-            q = q_ref[:, h * HD : (h + 1) * HD]
-            scores = lax.dot_general(
+        def one_head(h, carry):
+            q = q_ref[:, pl.ds(pl.multiple_of(h * HD, HD), HD)]
+            raw = lax.dot_general(
                 q, k, (((1,), (1,)), ((), ())), preferred_element_type=jnp.float32
-            ) * HD ** (-0.5)
+            )
             if masked:
-                scores = jnp.where(allowed, scores, MASK_FILL)
+                raw = jnp.where(allowed, raw, MASK_FILL)
             top_old = top_sc[h]
-            top_new = jnp.maximum(top_old, jnp.max(scores, axis=1, keepdims=True))
-            weights = jnp.exp(scores - top_new)
-            if masked:
-                weights = jnp.where(allowed, weights, 0.0)
-            rescale = jnp.exp(top_old - top_new)
+            top_new = jnp.maximum(top_old, jnp.max(raw, axis=1, keepdims=True))
+            weights = jnp.exp2((raw - top_new) * EXP2_SCALE)
+            rescale = jnp.exp2((top_old - top_new) * EXP2_SCALE)
             sum_sc[h] = sum_sc[h] * rescale + jnp.sum(weights, axis=1, keepdims=True)
             update = lax.dot_general(
                 weights.astype(jnp.bfloat16),
@@ -80,6 +79,9 @@
             )
             acc_sc[h] = acc_sc[h] * rescale + update
             top_sc[h] = top_new
+            return carry
+
+        lax.fori_loop(0, groups, one_head, 0)
 
     @pl.when(needed & full)
     def _():
@@ -153,17 +155,16 @@
 def shards(queries, keys, values, doc_lengths):
     rows = keys.shape[0]
     heads = keys.shape[1] // HD
+    groups = queries.shape[1] // keys.shape[1]
+    half = groups // 2
     kv_pairs = jnp.concatenate(
         [keys.reshape(rows, heads, HD), values.reshape(rows, heads, HD)], axis=2
     )
     kv_loc = lax.all_to_all(kv_pairs, "head", split_axis=1, concat_axis=0, tiled=True)
     kv_loc = kv_loc.reshape(kv_loc.shape[0], 2 * HD)
-    q_loc = lax.all_to_all(
-        queries.reshape(rows, heads, -1), "head", split_axis=1, concat_axis=0, tiled=True
-    )
-    q_loc = q_loc.reshape(q_loc.shape[0], -1)
+    tokens = kv_loc.shape[0]
+    q_split = queries.reshape(rows, heads, groups, HD)
     my_index = lax.axis_index("ctx")
-    tokens = q_loc.shape[0]
     doc_ends = jnp.cumsum(doc_lengths)
     doc_starts = doc_ends - doc_lengths
     row_pos = my_index * tokens + jnp.arange(tokens, dtype=jnp.int32)
@@ -174,11 +175,17 @@
     kv_all = jnp.concatenate(pieces[::-1], axis=0)
     q_base = (my_index * tokens).astype(jnp.int32)
     k_base = ((my_index - REACH) * tokens).astype(jnp.int32)
-    owned = attend(q_loc, kv_all, row_low, q_base, k_base)
-    back = lax.all_to_all(
-        owned.reshape(heads, rows, -1), "head", split_axis=0, concat_axis=0, tiled=True
-    )
-    return jnp.transpose(back, (1, 0, 2)).reshape(rows, -1)
+    returned = []
+    for first in range(0, groups, half):
+        q_part = q_split[:, :, first : first + half, :].reshape(rows, heads, half * HD)
+        q_loc = lax.all_to_all(q_part, "head", split_axis=1, concat_axis=0, tiled=True)
+        owned = attend(q_loc.reshape(tokens, half * HD), kv_all, row_low, q_base, k_base)
+        back = lax.all_to_all(
+            owned.reshape(heads, rows, half * HD), "head", split_axis=0, concat_axis=0, tiled=True
+        )
+        returned.append(back.reshape(heads, rows, half, HD))
+    joined = jnp.concatenate(returned, axis=2)
+    return jnp.transpose(joined, (1, 0, 2, 3)).reshape(rows, -1)
 
 
 def solution(mesh):

time: 182 us -> 185 us (1.016)
  the two profiles are of different devices: /device:TPU:32 before, /device:TPU:96 now
where the time goes in v1:
time: 185 us; the launch traced here: 184 us
  Pallas kernels  86.7 us (47%)
  waiting for transfers between devices  48.5 us (26%)
  starting transfers between devices  30.9 us (17%)
  local copies, waits for them, and re-layouts  12.4 us (7%)
  other arithmetic  5.54 us (3%)
    pallas_call x2, Pallas kernels, attend(): pl.pallas_call(functools.partial(attention_kernel, groups=groups), grid_s...  86.7 us
    ppermute x3, waiting for transfers between devices, shifted(): return lax.ppermute(block, axis, route)  22 us
    all_to_all x2, waiting for transfers between devices, shards(): lax.all_to_all(owned.reshape(heads, rows, half * HD), 'head', split_axis=...  15.7 us
    ppermute x3, starting transfers between devices, shifted(): return lax.ppermute(block, axis, route)  10.2 us
    all_to_all x2, starting transfers between devices, shards(): lax.all_to_all(owned.reshape(heads, rows, half * HD), 'head', split_axis=...  9.27 us
    all_to_all x1, waiting for transfers between devices, shards(): lax.all_to_all(kv_pairs, 'head', split_axis=1, concat_axis=0, tiled=True)  7.37 us
    all_to_all x2, starting transfers between devices, shards(): lax.all_to_all(q_part, 'head', split_axis=1, concat_axis=0, tiled=True)  7.12 us
    unnamed x12, local copies, waits for them, and re-layouts  4.69 us
  transfers between devices with their start and end apart: 8, of which 5 were waited for; matrix products, arithmetic and copies ran while one was open for 5% of the time, Pallas kernels for 47%

profile of v1, /device:TPU:96, one launch (start us, length us, event | category | flops | bytes accessed | tf_op | source)
XLA Modules:
  0.0 184.3 jit_solution(7898724941148123696)
XLA Ops:
  0.0 0.0 copy-start
  0.0 0.0 copy-start.3
  0.0 0.9 copy-done
  1.0 1.1 copy_bitcast_fusion.1
  2.0 0.9 pad_maximum_fusion.2
  2.9 4.3 %all-to-all-start.1 = ((bf16[128,8,256]{2,0,1:T(8,128)(2,1)}), bf16[128,8,256]{2,0,1:T(8,128)(2,1)}, u32[]{:S(2)}, u32[]{:S(2)}) async-start(bf16[128,8,256]{2,0,1:T(8,128)(2,1)} %pad_maximum_fusion.2), calls=%async_computation.1 | async-start | bytes 1048576 | tf_op jit(solution)/shard_map/all_to_all | solution.py:163
  7.2 0.0 copy-done.3
  7.2 0.6 copy.35
  7.8 0.7 fusion.2
  8.5 0.4 reshape.218
  9.0 0.0 copy-start.4
  9.0 1.3 copy.31
  10.3 7.4 %all-to-all-done.1 = bf16[128,8,256]{2,0,1:T(8,128)(2,1)} async-done(((bf16[128,8,256]{2,0,1:T(8,128)(2,1)}), bf16[128,8,256]{2,0,1:T(8,128)(2,1)}, u32[]{:S(2)}, u32[]{:S(2)}) %all-to-all-start.1) | async-done | bytes 524320 | tf_op jit(solution)/shard_map/all_to_all | solution.py:163
  17.6 3.6 %all-to-all-start.3 = ((bf16[128,8,512]{2,0,1:T(8,128)(2,1)}), bf16[128,8,512]{2,0,1:T(8,128)(2,1)S(1)}, u32[]{:S(2)}, u32[]{:S(2)}) async-start(bf16[128,8,512]{2,0,1:T(8,128)(2,1)} %copy.31), calls=%async_computation.3 | async-start | bytes 2097152 | tf_op jit(solution)/shard_map/all_to_all | solution.py:181
  21.2 0.0 copy-done.4
  21.2 0.2 reduce-window.9
  21.4 0.1 select_reduce_fusion
  21.5 0.1 slice.15
  21.6 0.1 slice.14
  21.7 0.4 reshape.217
  22.1 1.3 copy.30
  23.4 3.5 %collective-permute-start.2 = (bf16[1024,256]{1,0:T(8,128)(2,1)}, bf16[1024,256]{1,0:T(8,128)(2,1)S(1)}, u32[]{:S(2)}, u32[]{:S(2)}) collective-permute-start(bf16[1024,256]{1,0:T(8,128)(2,1)} %bitcast.11), channel_id=1, source_target_pairs={{0,8},{8,16},{16,24},{24,32},{32,40},{40,48},{48,56},{56,64},{64,7... | collective-permute-start | bytes 1572872 | tf_op jit(solution)/shard_map/ppermute | solution.py:23
  26.9 4.8 %collective-permute-start.1 = (bf16[1024,256]{1,0:T(8,128)(2,1)}, bf16[1024,256]{1,0:T(8,128)(2,1)S(1)}, u32[]{:S(2)}, u32[]{:S(2)}) collective-permute-start(bf16[1024,256]{1,0:T(8,128)(2,1)} %bitcast.11), channel_id=1, source_target_pairs={{0,16},{8,24},{16,32},{24,40},{32,48},{40,56},{48,64},{56,72},{64,... | collective-permute-start | bytes 1572872 | tf_op jit(solution)/shard_map/ppermute | solution.py:23
  31.7 1.9 %collective-permute-start = (bf16[1024,256]{1,0:T(8,128)(2,1)}, bf16[1024,256]{1,0:T(8,128)(2,1)}, u32[]{:S(2)}, u32[]{:S(2)}) collective-permute-start(bf16[1024,256]{1,0:T(8,128)(2,1)} %bitcast.11), channel_id=1, source_target_pairs={{0,24},{8,32},{16,40},{24,48},{32,56},{40,64},{48,72},{56,80},{64,... | collective-permute-start | bytes 1572872 | tf_op jit(solution)/shard_map/ppermute | solution.py:23
  33.7 3.4 %all-to-all-done.3 = bf16[128,8,512]{2,0,1:T(8,128)(2,1)S(1)} async-done(((bf16[128,8,512]{2,0,1:T(8,128)(2,1)}), bf16[128,8,512]{2,0,1:T(8,128)(2,1)S(1)}, u32[]{:S(2)}, u32[]{:S(2)}) %all-to-all-start.3) | async-done | bytes 1048608 | tf_op jit(solution)/shard_map/all_to_all | solution.py:181
  37.1 0.0 copy-start.1
  37.1 3.6 %all-to-all-start = ((bf16[128,8,512]{2,0,1:T(8,128)(2,1)}), bf16[128,8,512]{2,0,1:T(8,128)(2,1)S(1)}, u32[]{:S(2)}, u32[]{:S(2)}) async-start(bf16[128,8,512]{2,0,1:T(8,128)(2,1)} %copy.30), calls=%async_computation | async-start | bytes 2097152 | tf_op jit(solution)/shard_map/all_to_all | solution.py:181
  40.7 0.1 copy.21
  40.8 0.1 reshape.202
  40.9 1.0 copy.25.low_ref
  41.9 0.6 pad_add_fusion.1.table_ref
  42.5 0.0 collective-permute-done.2
  42.5 16.4 %collective-permute-done.1 = bf16[1024,256]{1,0:T(8,128)(2,1)S(1)} collective-permute-done((bf16[1024,256]{1,0:T(8,128)(2,1)}, bf16[1024,256]{1,0:T(8,128)(2,1)S(1)}, u32[]{:S(2)}, u32[]{:S(2)}) %collective-permute-start.1) | collective-permute-done | bytes 524320 | tf_op jit(solution)/shard_map/ppermute | solution.py:23
  59.0 5.6 %collective-permute-done = bf16[1024,256]{1,0:T(8,128)(2,1)} collective-permute-done((bf16[1024,256]{1,0:T(8,128)(2,1)}, bf16[1024,256]{1,0:T(8,128)(2,1)}, u32[]{:S(2)}, u32[]{:S(2)}) %collective-permute-start) | collective-permute-done | bytes 524320 | tf_op jit(solution)/shard_map/ppermute | solution.py:23
  64.6 2.7 %pad_maximum_fusion.k_ref.v_ref = bf16[4096,256]{1,0:T(8,128)(2,1)} fusion(bf16[1024,256]{1,0:T(8,128)(2,1)} %bitcast.11, bf16[1024,256]{1,0:T(8,128)(2,1)S(1)} %collective-permute-done.2, bf16[1024,256]{1,0:T(8,128)(2,1)S(1)} %collective-permute-done.1, bf16[1024,256]{1,0:T(8,128)(2,1)} %collective-permute-done), kind=kLoop, calls=%fused_computation.1 | loop fusion | flops 8388608 | bytes 4194304 | tf_op jit(solution)/shard_map/concatenate | solution.py:175
  67.2 0.0 copy-done.1
  67.2 43.4 %shard_map.47 = bf16[1024,512]{1,0:T(8,128)(2,1)} custom-call(s32[10]{0:T(128)} %pad_add_fusion.1.table_ref, bf16[1024,512]{1,0:T(8,128)(2,1)} %bitcast.48, bf16[4096,256]{1,0:T(8,128)(2,1)} %pad_maximum_fusion.k_ref.v_ref, bf16[4096,256]{1,0:T(8,128)(2,1)} %pad_maximum_fusion.k_ref.v_ref, s32[1024,1]{1,0:T(8,128)} %copy.25.low_ref), custom_call_target="tpu_custom_call" | custom-call | tf_op jit(solution)/shard_map/pallas_call | solution.py:145
  110.6 0.0 all-to-all-done
  110.6 0.0 copy-start.2
  110.6 4.5 %all-to-all-start.4 = ((bf16[8,128,512]{2,1,0:T(8,128)(2,1)}), bf16[8,128,512]{2,1,0:T(8,128)(2,1)S(1)}, u32[]{:S(2)}, u32[]{:S(2)}) async-start(bf16[8,128,512]{2,1,0:T(8,128)(2,1)} %bitcast.50), calls=%async_computation.4 | async-start | bytes 2097152 | tf_op jit(solution)/shard_map/all_to_all | solution.py:183
  115.1 0.0 copy-done.2
  115.1 43.4 %shard_map.46 = bf16[1024,512]{1,0:T(8,128)(2,1)} custom-call(s32[10]{0:T(128)} %pad_add_fusion.1.table_ref, bf16[1024,512]{1,0:T(8,128)(2,1)} %bitcast.49, bf16[4096,256]{1,0:T(8,128)(2,1)} %pad_maximum_fusion.k_ref.v_ref, bf16[4096,256]{1,0:T(8,128)(2,1)} %pad_maximum_fusion.k_ref.v_ref, s32[1024,1]{1,0:T(8,128)} %copy.25.low_ref), custom_call_target="tpu_custom_call" | custom-call | tf_op jit(solution)/shard_map/pallas_call | solution.py:145
  158.5 0.0 all-to-all-done.4
  158.5 4.8 %all-to-all-start.2 = ((bf16[8,128,512]{2,1,0:T(8,128)(2,1)}), bf16[8,128,512]{2,1,0:T(8,128)(2,1)S(1)}, u32[]{:S(2)}, u32[]{:S(2)}) async-start(bf16[8,128,512]{2,1,0:T(8,128)(2,1)} %bitcast.51), calls=%async_computation.2 | async-start | bytes 2097152 | tf_op jit(solution)/shard_map/all_to_all | solution.py:183
  163.3 0.3 reshape.215
  163.5 15.7 %all-to-all-done.2 = bf16[8,128,512]{2,1,0:T(8,128)(2,1)S(1)} async-done(((bf16[8,128,512]{2,1,0:T(8,128)(2,1)}), bf16[8,128,512]{2,1,0:T(8,128)(2,1)S(1)}, u32[]{:S(2)}, u32[]{:S(2)}) %all-to-all-start.2) | async-done | bytes 1048608 | tf_op jit(solution)/shard_map/all_to_all | solution.py:183
  179.2 0.3 reshape.211
  179.5 1.1 pad_maximum_fusion.1
  180.6 0.6 copy.32
  181.2 3.1 %copy.40 = bf16[16,8,64,128]{3,1,2,0:T(8,128)(2,1)} copy(bf16[16,8,64,128]{3,2,1,0:T(8,128)(2,1)S(1)} %bitcast.47) | data formatting | bytes 4194304
  (5 shorter events, 0.0 us)
Async XLA Ops:
  0.0 1.0 copy-start
  0.0 7.2 %copy-start.3 = (bf16[128,8192]{1,0:T(8,128)(2,1)S(1)}, bf16[128,8192]{1,0:T(8,128)(2,1)}, u32[]{:S(2)}) copy-start(bf16[128,8192]{1,0:T(8,128)(2,1)} %param.4) | copy-start | bytes 6291460
  2.9 14.8 %all-to-all-start.1 = ((bf16[128,8,256]{2,0,1:T(8,128)(2,1)}), bf16[128,8,256]{2,0,1:T(8,128)(2,1)}, u32[]{:S(2)}, u32[]{:S(2)}) async-start(bf16[128,8,256]{2,0,1:T(8,128)(2,1)} %pad_maximum_fusion.2), calls=%async_computation.1 | async-start | bytes 1048576 | tf_op jit(solution)/shard_map/all_to_all | solution.py:163
  9.0 12.2 %copy-start.4 = (s32[8]{0:T(128)S(1)}, s32[8]{0:T(128)}, u32[]{:S(2)}) copy-start(s32[8]{0:T(128)} %param.7) | copy-start | bytes 100
  17.6 19.5 %all-to-all-start.3 = ((bf16[128,8,512]{2,0,1:T(8,128)(2,1)}), bf16[128,8,512]{2,0,1:T(8,128)(2,1)S(1)}, u32[]{:S(2)}, u32[]{:S(2)}) async-start(bf16[128,8,512]{2,0,1:T(8,128)(2,1)} %copy.31), calls=%async_computation.3 | async-start | bytes 2097152 | tf_op jit(solution)/shard_map/all_to_all | solution.py:181
  23.4 19.1 %collective-permute-start.2 = (bf16[1024,256]{1,0:T(8,128)(2,1)}, bf16[1024,256]{1,0:T(8,128)(2,1)S(1)}, u32[]{:S(2)}, u32[]{:S(2)}) collective-permute-start(bf16[1024,256]{1,0:T(8,128)(2,1)} %bitcast.11), channel_id=1, source_target_pairs={{0,8},{8,16},{16,24},{24,32},{32,40},{40,48},{48,56},{56,64},{64,7... | collective-permute-start | bytes 1572872 | tf_op jit(solution)/shard_map/ppermute | solution.py:23
  26.9 32.1 %collective-permute-start.1 = (bf16[1024,256]{1,0:T(8,128)(2,1)}, bf16[1024,256]{1,0:T(8,128)(2,1)S(1)}, u32[]{:S(2)}, u32[]{:S(2)}) collective-permute-start(bf16[1024,256]{1,0:T(8,128)(2,1)} %bitcast.11), channel_id=1, source_target_pairs={{0,16},{8,24},{16,32},{24,40},{32,48},{40,56},{48,64},{56,72},{64,... | collective-permute-start | bytes 1572872 | tf_op jit(solution)/shard_map/ppermute | solution.py:23
  31.7 32.9 %collective-permute-start = (bf16[1024,256]{1,0:T(8,128)(2,1)}, bf16[1024,256]{1,0:T(8,128)(2,1)}, u32[]{:S(2)}, u32[]{:S(2)}) collective-permute-start(bf16[1024,256]{1,0:T(8,128)(2,1)} %bitcast.11), channel_id=1, source_target_pairs={{0,24},{8,32},{16,40},{24,48},{32,56},{40,64},{48,72},{56,80},{64,... | collective-permute-start | bytes 1572872 | tf_op jit(solution)/shard_map/ppermute | solution.py:23
  37.1 30.1 %copy-start.1 = (bf16[128,8,512]{2,0,1:T(8,128)(2,1)}, bf16[128,8,512]{2,0,1:T(8,128)(2,1)S(1)}, u32[]{:S(2)}) copy-start(bf16[128,8,512]{2,0,1:T(8,128)(2,1)S(1)} %all-to-all-done.3) | copy-start | bytes 3145732
  37.1 73.5 %all-to-all-start = ((bf16[128,8,512]{2,0,1:T(8,128)(2,1)}), bf16[128,8,512]{2,0,1:T(8,128)(2,1)S(1)}, u32[]{:S(2)}, u32[]{:S(2)}) async-start(bf16[128,8,512]{2,0,1:T(8,128)(2,1)} %copy.30), calls=%async_computation | async-start | bytes 2097152 | tf_op jit(solution)/shard_map/all_to_all | solution.py:181
  110.6 4.5 %copy-start.2 = (bf16[128,8,512]{2,0,1:T(8,128)(2,1)}, bf16[128,8,512]{2,0,1:T(8,128)(2,1)S(1)}, u32[]{:S(2)}) copy-start(bf16[128,8,512]{2,0,1:T(8,128)(2,1)S(1)} %all-to-all-done) | copy-start | bytes 3145732
  110.6 47.9 %all-to-all-start.4 = ((bf16[8,128,512]{2,1,0:T(8,128)(2,1)}), bf16[8,128,512]{2,1,0:T(8,128)(2,1)S(1)}, u32[]{:S(2)}, u32[]{:S(2)}) async-start(bf16[8,128,512]{2,1,0:T(8,128)(2,1)} %bitcast.50), calls=%async_computation.4 | async-start | bytes 2097152 | tf_op jit(solution)/shard_map/all_to_all | solution.py:183
  158.5 20.8 %all-to-all-start.2 = ((bf16[8,128,512]{2,1,0:T(8,128)(2,1)}), bf16[8,128,512]{2,1,0:T(8,128)(2,1)S(1)}, u32[]{:S(2)}, u32[]{:S(2)}) async-start(bf16[8,128,512]{2,1,0:T(8,128)(2,1)} %bitcast.51), calls=%async_computation.2 | async-start | bytes 2097152 | tf_op jit(solution)/shard_map/all_to_all | solution.py:183
